TPU v7x, 32 devices: a whole 2x2x4 slice. The times are simulated.
32 devices in a mesh: img: 4 (over y, core), slab: 8 (over z, x).
Axes of the slice: x: 2, y: 2, z: 4, core: 2. Of those that a mesh axis runs over, the one named last changes fastest.
Arguments:
- images: bfloat16 [32, 400, 400], P(('img', 'slab')), may hold values from -1500 to 1500, as said below
- micrograph: int32 [32], P(('img', 'slab')), may hold values from 0 to 63
- defocus: float32 [64], replicated, may hold values from 30 to 90
- target_slab: int32 [32, 8, 1], P(('img', 'slab')), may hold values from 0 to 7; in each aligned block of 8 rows (0 to 7, 8 to 15, ..., all dimensions but the last counted through in order) at most 2 rows name the same one
- target_plane: int32 [32, 8], P(('img', 'slab')), may hold values from 0 to 1
- target_rows: int32 [32, 8], P(('img', 'slab')), may hold values from 0 to 7
- shift_index: int32 [32, 8], P(('img', 'slab')), may hold values from 0 to 7
- volume: bfloat16 [16, 128, 800], P('slab'), may hold values from -6 to 6
Outputs:
- residual: bfloat16 [32, 400, 400], P(('img', 'slab'))
- reconstruction: float32 [16, 128, 800], P('slab', 'img')
Inputs may be any that keep to these rules, and one draw needn't show every extreme that they name: `target_slab`: in the 8 routed blocks of one device (aligned blocks of rows, particle by particle), no slab is named more than 2 times, a bound that some block reaches. `images`: real pixel values.
All inputs are finite; a program needn't handle non-finite values.
Results may differ from a plain program's by a relative error of at most 0.013.
Values may be sent and summed in bfloat16 or wider, within the bound.
No kernel may reach another device: no remote copies, remote signals or barrier semaphores. Data moves between devices by JAX's collectives and lax.ppermute only.
A program may use at most 128 MiB of HBM per device.

v0:
```python
import math
import jax
import jax.numpy as jnp
from jax import lax
from jax.sharding import PartitionSpec as P

RB = 16
LOW = 4
WL = 8


def dft_tables(box_size):
    positions = jnp.arange(box_size, dtype=jnp.int32)
    phase_steps = positions[:, None] * positions[None, :] % box_size
    angles = phase_steps.astype(jnp.float32) * (2.0 * math.pi / box_size)
    return (jnp.cos(angles).astype(jnp.bfloat16), jnp.sin(angles).astype(jnp.bfloat16))


def forward_tables(cosine_table, sine_table):
    right_table = jnp.concatenate([cosine_table, -sine_table], axis=1)
    left_table = jnp.stack(
        [jnp.stack([cosine_table, sine_table]), jnp.stack([-sine_table, cosine_table])]
    )
    return (right_table, left_table)


def inverse_tables(cosine_table, sine_table):
    upper_half = jnp.concatenate([cosine_table, sine_table], axis=1)
    lower_half = jnp.concatenate([-sine_table, cosine_table], axis=1)
    back_table = jnp.concatenate([upper_half, lower_half], axis=0)
    final_table = jnp.stack([cosine_table, -sine_table])
    return (back_table, final_table)


def transform(image_block, right_table, left_table):
    batch_size, box_size = (image_block.shape[0], image_block.shape[1])
    rowwise = jnp.einsum(
        "nyx,xm->nym", image_block, right_table, preferred_element_type=jnp.float32
    ).astype(jnp.bfloat16)
    quarters = rowwise.reshape(batch_size, box_size, 2, box_size)
    spectrum = jnp.einsum(
        "ahky,nyhm->nkam", left_table, quarters, preferred_element_type=jnp.float32
    )
    return spectrum.reshape(batch_size, box_size, 2 * box_size)


def invert(difference, back_table, final_table):
    batch_size, box_size = (difference.shape[0], difference.shape[1])
    rowwise = jnp.einsum(
        "nyj,jk->nyk", difference, back_table, preferred_element_type=jnp.float32
    ).astype(jnp.bfloat16)
    quarters = rowwise.reshape(batch_size, box_size, 2, box_size)
    picture = (
        jnp.einsum("cxk,nkcm->nxm", final_table, quarters, preferred_element_type=jnp.float32)
        / box_size
    )
    return picture.astype(jnp.bfloat16)


def radius_sq(row_ids, box_size):
    half_size = box_size // 2
    columns = jnp.arange(box_size, dtype=jnp.int32)
    freq_rows = jnp.where(row_ids < half_size, row_ids, row_ids - box_size)
    freq_cols = jnp.where(columns < half_size, columns, columns - box_size)
    total = freq_rows[..., None] * freq_rows[..., None] + freq_cols * freq_cols
    return total.astype(jnp.float32) / float(half_size * half_size)


def contrast_curve(defocus_of, row_ids, box_size):
    radius = radius_sq(row_ids, box_size)
    return (-jnp.sin(defocus_of[:, None, None] * radius + 0.1)).astype(jnp.bfloat16)


def lookup_defocus(mic_ids, defocus):
    labels = jnp.arange(defocus.shape[0], dtype=jnp.int32)
    return jnp.sum(jnp.where(mic_ids[:, None] == labels[None, :], defocus[None, :], 0.0), axis=1)


def shift_halves(values, steps, box_size):
    split_shape = values.shape[:-1] + (2, box_size)
    return jnp.roll(values.reshape(split_shape), steps, axis=-1).reshape(values.shape)


def body(images, micrograph, defocus, target_slab, target_plane, target_rows, shift_index, volume):
    particles, box_size = (images.shape[0], images.shape[1])
    slab_count = lax.axis_size("slab")
    device_count = lax.axis_size("img") * slab_count
    low_rows = LOW * RB
    routed = particles * 2 * LOW
    cosine_table, sine_table = dft_tables(box_size)
    right_table, left_table = forward_tables(cosine_table, sine_table)
    back_table, final_table = inverse_tables(cosine_table, sine_table)
    spectrum = transform(images, right_table, left_table)
    real_part = spectrum[..., :box_size]
    imag_part = spectrum[..., box_size:]
    power_sum = jnp.sum(real_part * real_part + imag_part * imag_part, axis=0)
    power_all = lax.psum(power_sum, ("img", "slab"))
    noise_level = jnp.sqrt(power_all / (particles * device_count) + 1e-06)
    whitened = spectrum / jnp.concatenate([noise_level, noise_level], axis=1)
    row_all = jnp.arange(box_size, dtype=jnp.int32)[None, :]
    contrast = contrast_curve(lookup_defocus(micrograph, defocus), row_all, box_size)
    contrast_both = jnp.concatenate([contrast, contrast], axis=-1).astype(jnp.float32)
    weighted = (contrast_both * whitened).astype(jnp.bfloat16)
    low_blocks = jnp.concatenate(
        [weighted[:, :low_rows], weighted[:, box_size - low_rows :]], axis=1
    )
    low_blocks = low_blocks.reshape(routed, RB, 2 * box_size)
    destination = target_slab.reshape(routed)
    capacity = max(2, (2 * routed + slab_count - 1) // slab_count)
    member = (destination[:, None] == jnp.arange(slab_count, dtype=jnp.int32)[None, :]).astype(
        jnp.int32
    )
    before = jnp.cumsum(member, axis=0) - member
    slot_rank = jnp.sum(member * before, axis=1)
    seat_index = destination * capacity + slot_rank
    seat_count = slab_count * capacity
    live_flag = jnp.ones((routed,), jnp.int32)
    source_block = jnp.tile(jnp.arange(2 * LOW, dtype=jnp.int32), particles)
    block_info = jnp.stack(
        [
            live_flag,
            target_plane.reshape(routed),
            target_rows.reshape(routed),
            shift_index.reshape(routed),
            source_block,
            jnp.repeat(micrograph, 2 * LOW),
        ],
        axis=1,
    )
    send_blocks = (
        jnp.zeros((seat_count, RB, 2 * box_size), jnp.bfloat16).at[seat_index].set(low_blocks)
    )
    send_info = jnp.zeros((seat_count, 6), jnp.int32).at[seat_index].set(block_info)
    low_contrast = jnp.concatenate(
        [contrast[:, :low_rows], contrast[:, box_size - low_rows :]], axis=1
    )
    low_contrast = low_contrast.reshape(routed, RB, box_size)
    send_contrast = (
        jnp.zeros((seat_count, RB, box_size), jnp.bfloat16).at[seat_index].set(low_contrast)
    )
    got_blocks, got_contrast, got_info = (
        lax.all_to_all(send_blocks, "slab", split_axis=0, concat_axis=0, tiled=True),
        lax.all_to_all(send_contrast, "slab", split_axis=0, concat_axis=0, tiled=True),
        lax.all_to_all(send_info, "slab", split_axis=0, concat_axis=0, tiled=True),
    )
    live_mask = got_info[:, 0].astype(jnp.float32)[:, None, None]
    row_index = got_info[:, 2][:, None] * RB + jnp.arange(RB, dtype=jnp.int32)
    plane_index = jnp.broadcast_to(got_info[:, 1][:, None], row_index.shape)
    blend_weight = ((got_info[:, 3].astype(jnp.float32) + 0.5) / WL)[:, None, None]
    nearby = volume[plane_index, row_index].astype(jnp.float32)
    projected = (
        ((1.0 - blend_weight) * nearby + blend_weight * shift_halves(nearby, -1, box_size))
        * live_mask
    ).astype(jnp.bfloat16)
    returned_rows = lax.all_to_all(projected, "slab", split_axis=0, concat_axis=0, tiled=True)
    received = got_blocks.astype(jnp.float32)
    inserted = (1.0 - blend_weight) * received + blend_weight * shift_halves(received, 1, box_size)
    contrast_rows = got_contrast.astype(jnp.float32)
    squared = contrast_rows * contrast_rows
    weights = (1.0 - blend_weight) * squared + blend_weight * jnp.roll(squared, 1, axis=-1)
    numerator = jnp.zeros((volume.shape[0], volume.shape[1], 3 * box_size), jnp.float32)
    numerator = numerator.at[plane_index, row_index].add(
        jnp.concatenate([inserted, weights], axis=-1) * live_mask
    )
    volume_part = lax.psum_scatter(
        numerator.astype(jnp.bfloat16), "img", scatter_dimension=1, tiled=True
    ).astype(jnp.float32)
    weight_sum = volume_part[..., 2 * box_size :]
    reconstruction = volume_part[..., : 2 * box_size] / (
        jnp.concatenate([weight_sum, weight_sum], axis=-1) + 1.0
    )
    own_rows = returned_rows[seat_index].reshape(particles, 2 * low_rows, 2 * box_size)
    middle = jnp.zeros((particles, box_size - 2 * low_rows, 2 * box_size), jnp.bfloat16)
    full_projection = jnp.concatenate(
        [own_rows[:, :low_rows], middle, own_rows[:, low_rows:]], axis=1
    )
    difference = (whitened - contrast_both * full_projection.astype(jnp.float32)).astype(
        jnp.bfloat16
    )
    residual = invert(difference, back_table, final_table)
    return (residual, reconstruction)


def solution(mesh):
    in_specs = (
        P(("img", "slab"), None, None),
        P(("img", "slab")),
        P(),
        P(("img", "slab"), None, None),
        P(("img", "slab"), None),
        P(("img", "slab"), None),
        P(("img", "slab"), None),
        P("slab", None, None),
    )
    out_specs = (P(("img", "slab"), None, None), P("slab", "img", None))
    return jax.shard_map(body, mesh=mesh, in_specs=in_specs, out_specs=out_specs, check_vma=False)
```

profile of v0, /device:TPU:0, one launch (start us, length us, event | category | flops | bytes accessed | tf_op | source)
XLA Modules:
  0.0 247.4 jit_solution(15363540202320379219)
XLA Ops:
  7.2 3.5 %sine_convert_fusion = (bf16[1,400,400]{2,1,0:T(8,128)(2,1)S(1)}, bf16[1,400,400]{2,1,0:T(8,128)(2,1)S(1)}) fusion(), kind=kLoop, calls=%fused_computation.54 | loop fusion | flops 1760000 | bytes 640000 | tf_op jit(solution)/shard_map/convert_element_type | solution.py:16
  10.7 3.2 %fusion.52 = bf16[1,400,400]{2,1,0:T(8,128)(2,1)S(1)} fusion(), kind=kLoop, calls=%fused_computation.85 | loop fusion | flops 2080000 | bytes 320000 | tf_op jit(solution)/shard_map/neg | solution.py:20
  13.9 3.2 %cosine_convert_fusion.1 = bf16[400,400]{1,0:T(8,128)(2,1)S(1)} fusion(), kind=kLoop, calls=%fused_computation.60 | loop fusion | flops 1600000 | bytes 320000 | tf_op jit(solution)/shard_map/convert_element_type | solution.py:16
  17.1 3.2 %fusion.51 = bf16[400,400]{1,0:T(8,128)(2,1)S(1)} fusion(), kind=kLoop, calls=%fused_computation.84 | loop fusion | flops 2080000 | bytes 320000 | tf_op jit(solution)/shard_map/neg | solution.py:20
  29.9 7.3 %all-to-all-start = ((s32[8,2,6]{2,1,0:T(2,128)}), s32[8,2,6]{2,1,0:T(2,128)S(1)}, u32[]{:S(2)}, u32[]{:S(2)}) async-start(s32[8,2,6]{2,1,0:T(2,128)} %bitcast.23), calls=%async_computation | async-start | bytes 16384 | tf_op jit(solution)/shard_map/all_to_all | solution.py:144
  38.3 3.8 %fusion.53 = (bf16[1,400,400]{2,1,0:T(8,128)(2,1)}, bf16[400,400]{1,0:T(8,128)(2,1)}) fusion(f32[]{:T(128)S(6)} %mul.305, s32[400]{0:T(512)S(1)} %fusion.65), kind=kLoop, calls=%fused_computation.89 | loop fusion | flops 960000 | bytes 641604 | tf_op jit(solution)/shard_map/concatenate | solution.py:102
  42.1 3.0 %negate_convert_fusion = bf16[1,400,400]{2,1,0:T(8,128)(2,1)S(1)} fusion(f32[]{:T(128)S(6)} %mul.305, s32[400]{0:T(512)S(1)} %fusion.65), kind=kLoop, calls=%fused_computation.51 | loop fusion | flops 960000 | bytes 321604 | tf_op jit(solution)/shard_map/convert_element_type | solution.py:71
  45.5 3.1 %copy.28 = f32[400,800]{1,0:T(8,128)} copy(f32[400,800]{0,1:T(8,128)} %bitcast.75) | data formatting | bytes 2560000 | tf_op jit(solution)/shard_map/reshape | solution.py:44
  49.3 2.1 scatter_fusion.1
  51.4 6.0 %all-to-all-start.3 = ((bf16[16,16,400]{2,1,0:T(8,128)(2,1)}), bf16[16,16,400]{2,1,0:T(8,128)(2,1)}, u32[]{:S(2)}, u32[]{:S(2)}) async-start(bf16[16,16,400]{2,1,0:T(8,128)(2,1)} %scatter_fusion.1), calls=%async_computation.3 | async-start | bytes 524288 | tf_op jit(solution)/shard_map/all_to_all | solution.py:143
  57.8 2.7 %gather_fusion = bf16[256,800]{1,0:T(8,128)(2,1)S(1)} fusion(bf16[2,128,800]{2,1,0:T(8,128)(2,1)S(1)} %copy.30, s32[256]{0:T(256)S(1)} %reshape.583), kind=kCustom, calls=%fused_computation | custom fusion | bytes 821248 | tf_op jit(solution)/shard_map/gather | solution.py:150
  63.7 94.8 %all-reduce.2.cloned.1.call-done = f32[400,400]{1,0:T(8,128)} async-done(((f32[400,400]{1,0:T(8,128)}), f32[400,400]{1,0:T(8,128)}) %all-reduce.2.cloned.1.call-update) | async-done | bytes 640016 | tf_op jit(solution)/shard_map/psum | solution.py:97
  158.5 2.4 fusion.73
  162.3 2.2 scatter_fusion
  164.4 5.8 %all-to-all-start.2 = ((bf16[16,16,800]{2,1,0:T(8,128)(2,1)}), bf16[16,16,800]{2,1,0:T(8,128)(2,1)}, u32[]{:S(2)}, u32[]{:S(2)}) async-start(bf16[16,16,800]{2,1,0:T(8,128)(2,1)} %scatter_fusion), calls=%async_computation.2 | async-start | bytes 917504 | tf_op jit(solution)/shard_map/all_to_all | solution.py:142
  174.5 2.0 fusion.48
  176.5 5.8 %all-to-all-done.2 = bf16[16,16,800]{2,1,0:T(8,128)(2,1)} async-done(((bf16[16,16,800]{2,1,0:T(8,128)(2,1)}), bf16[16,16,800]{2,1,0:T(8,128)(2,1)}, u32[]{:S(2)}, u32[]{:S(2)}) %all-to-all-start.2) | async-done | bytes 409632 | tf_op jit(solution)/shard_map/all_to_all | solution.py:142
  182.4 2.3 reshape.579
  188.1 2.6 %multiply_add_fusion = (f32[16,16,800]{2,1,0:T(8,128)}, bf16[16,16,800]{2,1,0:T(8,128)(2,1)}) fusion(f32[16,16,800]{2,1,0:T(8,128)} %reshape.580, f32[16]{0:T(128)S(1)} %get-tuple-element.8, f32[16]{0:T(128)S(1)} %broadcast_subtract_fusion, bf16[16,16,800]{2,1,0:T(8,128)(2,1)} %all-to-all-done.2, f32[16]{0:T(128)S(1)} %get-tuple-element.9, ...), kind=kLoop, calls=%fused_computation.38 | loop fusion | flops 1843200 | bytes 4096192 | tf_op jit(solution)/shard_map/add | solution.py:157
  190.7 3.8 %all-to-all-start.1 = ((bf16[16,16,800]{2,1,0:T(8,128)(2,1)}), bf16[16,16,800]{2,1,0:T(8,128)(2,1)S(1)}, u32[]{:S(2)}, u32[]{:S(2)}) async-start(bf16[16,16,800]{2,1,0:T(8,128)(2,1)} %get-tuple-element.27), calls=%async_computation.1 | async-start | bytes 917504 | tf_op jit(solution)/shard_map/all_to_all | solution.py:155
  196.0 17.0 %scatter_fusion.2 = f32[2,128,1200]{2,1,0:T(8,128)S(1)} fusion(f32[2,128,1200]{2,1,0:T(8,128)S(1)} %broadcast_in_dim.29, s32[256]{0:T(256)S(1)} %reshape.621, f32[256,1200]{1,0:T(8,128)S(1)} %bitcast.77), kind=kCustom, calls=%fused_computation.5 | custom fusion | flops 307200 | bytes 3688448 | tf_op jit(solution)/shard_map/scatter-add | solution.py:162
  214.0 3.9 %sine_convert_fusion.1 = bf16[400,400]{1,0:T(8,128)(2,1)} fusion(), kind=kLoop, calls=%fused_computation.59 | loop fusion | flops 1600000 | bytes 320000 | tf_op jit(solution)/shard_map/convert_element_type | solution.py:16
  218.5 3.8 %fusion.16 = bf16[400,800]{1,0:T(8,128)(2,1)} fusion(bf16[400,400]{1,0:T(8,128)(2,1)} %copy-done.13, bf16[400,400]{1,0:T(8,128)(2,1)} %copy-done.14, bf16[400,400]{1,0:T(8,128)(2,1)} %sine_convert_fusion.1, f32[400,800]{1,0:T(8,128)S(1)} %copy-done.10, f32[400,400]{1,0:T(8,128)S(1)} %copy-done.11, bf16[400,400]{1,0:T(8,128)(2,1)} %get-tuple-element.23, ...), kind=kOutput, calls=%fused_computation.24 | convolution fusion | flops 522240000 | bytes 4045600 | tf_op jit(solution)/shard_map/nyj,jk->nyk/dot_general | solution.py:49
  225.4 12.5 %reduce-scatter.2.cloned.1.call-done = bf16[2,32,1200]{2,1,0:T(8,128)(2,1)} async-done(((bf16[2,128,1200]{2,1,0:T(8,128)(2,1)}), bf16[2,32,1200]{2,1,0:T(8,128)(2,1)}) %reduce-scatter.2.cloned.1.call-update) | async-done | bytes 153616 | tf_op jit(solution)/shard_map/reduce_scatter | solution.py:165
  (108 shorter events, 31.9 us)
Async XLA Ops:
  7.2 13.9 %copy-start = (bf16[1,400,400]{2,1,0:T(8,128)(2,1)S(1)}, bf16[1,400,400]{2,1,0:T(8,128)(2,1)}, u32[]{:S(2)}) copy-start(bf16[1,400,400]{2,1,0:T(8,128)(2,1)} %param.8) | copy-start | bytes 960004
  7.2 151.4 %all-reduce.2.cloned.1.call-start = ((), (), s32[]{:S(2)}) async-start(), calls=%async_computation.5 | async-start | bytes 1638400 | tf_op jit(solution)/shard_map/psum | solution.py:97
  10.7 12.3 %copy-start.6 = (bf16[1,400,400]{2,1,0:T(8,128)(2,1)}, bf16[1,400,400]{2,1,0:T(8,128)(2,1)S(1)}, u32[]{:S(2)}) copy-start(bf16[1,400,400]{2,1,0:T(8,128)(2,1)S(1)} %get-tuple-element.29) | copy-start | bytes 960004
  13.9 9.0 %copy-start.8 = (bf16[1,400,400]{2,1,0:T(8,128)(2,1)}, bf16[1,400,400]{2,1,0:T(8,128)(2,1)S(1)}, u32[]{:S(2)}) copy-start(bf16[1,400,400]{2,1,0:T(8,128)(2,1)S(1)} %fusion.52) | copy-start | bytes 960004
  17.1 3.2 %copy-start.13 = (bf16[400,400]{1,0:T(8,128)(2,1)}, bf16[400,400]{1,0:T(8,128)(2,1)S(1)}, u32[]{:S(2)}) copy-start(bf16[400,400]{1,0:T(8,128)(2,1)S(1)} %cosine_convert_fusion.1) | copy-start | bytes 960004
  26.3 1.9 copy-start.16
  26.3 2.3 copy-start.17
  26.3 2.3 copy-start.18
  26.3 2.3 copy-start.19
  26.3 10.8 %copy-start.20 = (f32[64]{0:T(128)S(1)}, f32[64]{0:T(128)}, u32[]{:S(2)}) copy-start(f32[64]{0:T(128)} %param.10) | copy-start | bytes 772
  27.5 17.7 %copy-start.15 = (bf16[2,128,800]{1,2,0:T(8,128)(2,1)S(1)}, bf16[2,128,800]{1,2,0:T(8,128)(2,1)}, u32[]{:S(2)}) copy-start(bf16[2,128,800]{1,2,0:T(8,128)(2,1)} %param.15) | copy-start | bytes 1228804
  29.9 21.6 %all-to-all-start = ((s32[8,2,6]{2,1,0:T(2,128)}), s32[8,2,6]{2,1,0:T(2,128)S(1)}, u32[]{:S(2)}, u32[]{:S(2)}) async-start(s32[8,2,6]{2,1,0:T(2,128)} %bitcast.23), calls=%async_computation | async-start | bytes 16384 | tf_op jit(solution)/shard_map/all_to_all | solution.py:144
  51.4 113.0 %all-to-all-start.3 = ((bf16[16,16,400]{2,1,0:T(8,128)(2,1)}), bf16[16,16,400]{2,1,0:T(8,128)(2,1)}, u32[]{:S(2)}, u32[]{:S(2)}) async-start(bf16[16,16,400]{2,1,0:T(8,128)(2,1)} %scatter_fusion.1), calls=%async_computation.3 | async-start | bytes 524288 | tf_op jit(solution)/shard_map/all_to_all | solution.py:143
  158.5 2.4 copy-start.5
  164.4 17.9 %all-to-all-start.2 = ((bf16[16,16,800]{2,1,0:T(8,128)(2,1)}), bf16[16,16,800]{2,1,0:T(8,128)(2,1)}, u32[]{:S(2)}, u32[]{:S(2)}) async-start(bf16[16,16,800]{2,1,0:T(8,128)(2,1)} %scatter_fusion), calls=%async_computation.2 | async-start | bytes 917504 | tf_op jit(solution)/shard_map/all_to_all | solution.py:142
  186.2 2.0 copy-start.2
  186.2 1.9 copy-start.3
  190.7 3.9 %copy-start.4 = (f32[16,16,800]{2,1,0:T(8,128)S(1)}, f32[16,16,800]{2,1,0:T(8,128)}, u32[]{:S(2)}) copy-start(f32[16,16,800]{2,1,0:T(8,128)} %get-tuple-element.26) | copy-start | bytes 2457604
  190.7 27.1 %all-to-all-start.1 = ((bf16[16,16,800]{2,1,0:T(8,128)(2,1)}), bf16[16,16,800]{2,1,0:T(8,128)(2,1)S(1)}, u32[]{:S(2)}, u32[]{:S(2)}) async-start(bf16[16,16,800]{2,1,0:T(8,128)(2,1)} %get-tuple-element.27), calls=%async_computation.1 | async-start | bytes 917504 | tf_op jit(solution)/shard_map/all_to_all | solution.py:155
  194.5 43.3 %reduce-scatter.2.cloned.1.call-start = ((), (), s32[]{:S(2)}) async-start(), calls=%async_computation.6 | async-start | bytes 819200 | tf_op jit(solution)/shard_map/reduce_scatter | solution.py:165
  213.0 5.5 %copy-start.11 = (f32[400,400]{1,0:T(8,128)S(1)}, f32[400,400]{1,0:T(8,128)}, u32[]{:S(2)}) copy-start(f32[400,400]{1,0:T(8,128)} %get-tuple-element.13) | copy-start | bytes 1920004
  213.9 4.5 %copy-start.10 = (f32[400,800]{1,0:T(8,128)S(1)}, f32[400,800]{1,0:T(8,128)}, u32[]{:S(2)}) copy-start(f32[400,800]{1,0:T(8,128)} %copy.28) | copy-start | bytes 3840004
  222.3 1.5 copy-start.7
  222.3 1.5 copy-start.9
  (3 other events, 3.1 us)
Sparse Core Ops, SparseCore 0:
  27.7 130.8 all-reduce.1
  214.1 23.7 reduce-scatter.1
where the time goes:
time: 248 us; the launch traced here: 247 us
  waiting for transfers between devices  113 us (46%)
  other arithmetic  58.7 us (24%)
  local copies, waits for them, and re-layouts  30.7 us (12%)
  starting transfers between devices  22.9 us (9%)
  between operations  15.8 us (6%)
  matrix products  6.11 us (2%)
    psum x1, waiting for transfers between devices, body(): power_all = lax.psum(power_sum, ('img', 'slab'))  94.8 us
    scatter-add x1, other arithmetic, body(): numerator.at[plane_index, row_index]  17 us
    reduce_scatter x1, waiting for transfers between devices, body(): lax.psum_scatter(numerator.astype(jnp.bfloat16), 'img', scatter_dimension...  12.5 us
    convert_element_type x2, other arithmetic, dft_tables(): jnp.sin(angles).astype(jnp.bfloat16)  7.32 us
    all_to_all x1, starting transfers between devices, body(): lax.all_to_all(send_info, 'slab', split_axis=0, concat_axis=0, tiled=True)  7.25 us
    neg x2, other arithmetic, forward_tables(): right_table = jnp.concatenate([cosine_table, -sine_table], axis=1)  6.42 us
    all_to_all x1, starting transfers between devices, body(): lax.all_to_all(send_contrast, 'slab', split_axis=0, concat_axis=0, tiled=...  5.99 us
    all_to_all x1, waiting for transfers between devices, body(): lax.all_to_all(send_blocks, 'slab', split_axis=0, concat_axis=0, tiled=True)  5.84 us
  transfers between devices with their start and end apart: 6, of which 3 were waited for; matrix products, arithmetic and copies ran while one was open for 26% of the time, Pallas kernels for 0%

commit v1 on v0

--- a/solution.py
+++ b/solution.py
@@ -94,7 +94,7 @@
     real_part = spectrum[..., :box_size]
     imag_part = spectrum[..., box_size:]
     power_sum = jnp.sum(real_part * real_part + imag_part * imag_part, axis=0)
-    power_all = lax.psum(power_sum, ("img", "slab"))
+    power_all = jnp.sum(lax.all_gather(power_sum, ("img", "slab")), axis=0)
     noise_level = jnp.sqrt(power_all / (particles * device_count) + 1e-06)
     whitened = spectrum / jnp.concatenate([noise_level, noise_level], axis=1)
     row_all = jnp.arange(box_size, dtype=jnp.int32)[None, :]

time: 248 us -> 314 us (1.27)
  waiting for transfers between devices: 113 us -> 150 us
  other arithmetic: 58.7 us -> 79.3 us
  local copies, waits for them, and re-layouts: 30.7 us -> 42 us
    all_gather x0 -> x1, waiting for transfers between devices: none -> 131 us  [body(): power_all = jnp.sum(lax.all_gather(power_sum, ('img', 'slab')), axis=0)]
    psum x1 -> x0, waiting for transfers between devices: 94.8 us -> none  [body(): power_all = lax.psum(power_sum, ('img', 'slab'))]
    scatter-add x1, other arithmetic: 17 us -> 27.9 us  [body(): numerator.at[plane_index, row_index]]
    reduce_sum x1, other arithmetic: 1.19 us -> 10.6 us  [body(): power_all = jnp.sum(lax.all_gather(power_sum, ('img', 'slab')), axis=0)]
    unnamed x44 -> x57, local copies, waits for them, and re-layouts: 3.65 us -> 7.76 us
    reshape x2 -> x0, local copies, waits for them, and re-layouts: 3.56 us -> none  [transform(): return spectrum.reshape(batch_size, box_size, 2 * box_size)]
  transfers between devices with their start and end apart: 6 -> 6, of which waited for: 3 -> 3; matrix products, arithmetic and copies ran while one was open for 26% -> 29% of each run, Pallas kernels for 0% -> 0%
where the time goes in v1:
time: 314 us; the launch traced here: 313 us
  waiting for transfers between devices  150 us (48%)
  other arithmetic  79.3 us (25%)
  local copies, waits for them, and re-layouts  42 us (13%)
  starting transfers between devices  21.9 us (7%)
  between operations  15.8 us (5%)
  matrix products  3.38 us (1%)
    all_gather x1, waiting for transfers between devices, body(): power_all = jnp.sum(lax.all_gather(power_sum, ('img', 'slab')), axis=0)  131 us
    scatter-add x1, other arithmetic, body(): numerator.at[plane_index, row_index]  27.9 us
    reduce_scatter x1, waiting for transfers between devices, body(): lax.psum_scatter(numerator.astype(jnp.bfloat16), 'img', scatter_dimension...  12.4 us
    reduce_sum x1, other arithmetic, body(): power_all = jnp.sum(lax.all_gather(power_sum, ('img', 'slab')), axis=0)  10.6 us
    unnamed x57, local copies, waits for them, and re-layouts  7.76 us
    convert_element_type x2, other arithmetic, dft_tables(): jnp.sin(angles).astype(jnp.bfloat16)  7.56 us
    all_to_all x1, starting transfers between devices, body(): lax.all_to_all(send_info, 'slab', split_axis=0, concat_axis=0, tiled=True)  7.25 us
    all_to_all x1, waiting for transfers between devices, body(): lax.all_to_all(send_blocks, 'slab', split_axis=0, concat_axis=0, tiled=True)  6.53 us
  transfers between devices with their start and end apart: 6, of which 3 were waited for; matrix products, arithmetic and copies ran while one was open for 29% of the time, Pallas kernels for 0%

profile of v1, /device:TPU:0, one launch (start us, length us, event | category | flops | bytes accessed | tf_op | source)
XLA Modules:
  0.0 312.5 jit_solution(1700866827599551254)
XLA Ops:
  7.2 3.5 %sine_convert_fusion = (bf16[1,400,400]{2,1,0:T(8,128)(2,1)S(1)}, bf16[1,400,400]{2,1,0:T(8,128)(2,1)S(1)}) fusion(), kind=kLoop, calls=%fused_computation.53 | loop fusion | flops 1760000 | bytes 640000 | tf_op jit(solution)/shard_map/convert_element_type | solution.py:16
  10.7 3.2 %fusion.42 = bf16[1,400,400]{2,1,0:T(8,128)(2,1)S(1)} fusion(), kind=kLoop, calls=%fused_computation.76 | loop fusion | flops 2080000 | bytes 320000 | tf_op jit(solution)/shard_map/neg | solution.py:20
  13.9 4.1 %sine_convert_fusion.1 = (bf16[400,400]{1,0:T(8,128)(2,1)}, bf16[400,400]{1,0:T(8,128)(2,1)S(1)}) fusion(), kind=kLoop, calls=%fused_computation.58 | loop fusion | flops 1760000 | bytes 640000 | tf_op jit(solution)/shard_map/convert_element_type | solution.py:16
  18.0 3.2 %fusion.41 = bf16[400,400]{1,0:T(8,128)(2,1)S(1)} fusion(), kind=kLoop, calls=%fused_computation.75 | loop fusion | flops 2080000 | bytes 320000 | tf_op jit(solution)/shard_map/neg | solution.py:20
  29.9 7.3 %all-to-all-start = ((s32[8,2,6]{2,1,0:T(2,128)}), s32[8,2,6]{2,1,0:T(2,128)S(1)}, u32[]{:S(2)}, u32[]{:S(2)}) async-start(s32[8,2,6]{2,1,0:T(2,128)} %bitcast.22), calls=%async_computation | async-start | bytes 16384 | tf_op jit(solution)/shard_map/all_to_all | solution.py:144
  38.4 3.0 negate_convert_fusion
  41.4 3.8 %fusion.43 = (bf16[1,400,400]{1,2,0:T(8,128)(2,1)}, bf16[400,400]{0,1:T(8,128)(2,1)}) fusion(f32[]{:T(128)S(6)} %mul.305, s32[400]{0:T(512)S(1)} %fusion.55), kind=kLoop, calls=%fused_computation.78 | loop fusion | flops 960000 | bytes 641604 | tf_op jit(solution)/shard_map/concatenate | solution.py:102
  48.3 6.0 %all-to-all-start.3 = ((bf16[16,16,400]{2,1,0:T(8,128)(2,1)}), bf16[16,16,400]{2,1,0:T(8,128)(2,1)}, u32[]{:S(2)}, u32[]{:S(2)}) async-start(bf16[16,16,400]{2,1,0:T(8,128)(2,1)} %scatter_fusion.1), calls=%async_computation.3 | async-start | bytes 524288 | tf_op jit(solution)/shard_map/all_to_all | solution.py:143
  54.7 3.4 %gather_fusion = bf16[256,800]{1,0:T(8,128)(2,1)} fusion(bf16[2,128,800]{2,1,0:T(8,128)(2,1)S(1)} %copy.37, s32[256]{0:T(256)S(1)} %reshape.575), kind=kCustom, calls=%fused_computation | custom fusion | bytes 821248 | tf_op jit(solution)/shard_map/gather | solution.py:150
  58.1 2.3 reshape.574
  63.6 131.1 %all-gather.2.cloned.1.call-done = f32[32,400,400]{2,1,0:T(8,128)} async-done(((f32[1,400,400]{2,1,0:T(8,128)}), f32[32,400,400]{2,1,0:T(8,128)}) %all-gather.2.cloned.1.call-update) | async-done | bytes 20480016 | tf_op jit(solution)/shard_map/all_gather | solution.py:97
  194.8 10.6 %reduce_sum.33 = f32[400,400]{1,0:T(8,128)} reduce(f32[32,400,400]{2,1,0:T(8,128)} %all-gather.2.cloned.1.call-done, f32[]{:T(128)} %constant.22.clone.1), dimensions={0}, to_apply=%region_0.1 | reduce | flops 4960000 | bytes 21120004 | tf_op jit(solution)/shard_map/reduce_sum | solution.py:97
  211.9 2.4 scatter_fusion
  214.3 4.3 %all-to-all-start.2 = ((bf16[16,16,800]{2,1,0:T(8,128)(2,1)}), bf16[16,16,800]{2,1,0:T(8,128)(2,1)}, u32[]{:S(2)}, u32[]{:S(2)}) async-start(bf16[16,16,800]{2,1,0:T(8,128)(2,1)} %scatter_fusion), calls=%async_computation.2 | async-start | bytes 917504 | tf_op jit(solution)/shard_map/all_to_all | solution.py:142
  220.4 3.2 %reshape.567 = f32[16,16,800]{2,1,0:T(8,128)} reshape(f32[16,16,2,400]{3,2,1,0:T(2,128)} %pad_maximum_fusion) | data formatting | bytes 1638400 | tf_op jit(solution)/shard_map/reshape | solution.py:81
  225.7 6.5 %all-to-all-done.2 = bf16[16,16,800]{2,1,0:T(8,128)(2,1)} async-done(((bf16[16,16,800]{2,1,0:T(8,128)(2,1)}), bf16[16,16,800]{2,1,0:T(8,128)(2,1)}, u32[]{:S(2)}, u32[]{:S(2)}) %all-to-all-start.2) | async-done | bytes 409632 | tf_op jit(solution)/shard_map/all_to_all | solution.py:142
  232.2 2.3 reshape.571
  234.9 2.1 pad_maximum_fusion.1
  237.0 3.2 %reshape.572 = f32[16,16,800]{2,1,0:T(8,128)} reshape(f32[16,16,2,400]{3,2,1,0:T(2,128)} %pad_maximum_fusion.1) | data formatting | bytes 1638400 | tf_op jit(solution)/shard_map/reshape | solution.py:81
  240.3 2.9 multiply_add_fusion
  243.2 4.2 %all-to-all-start.1 = ((bf16[16,16,800]{2,1,0:T(8,128)(2,1)}), bf16[16,16,800]{2,1,0:T(8,128)(2,1)}, u32[]{:S(2)}, u32[]{:S(2)}) async-start(bf16[16,16,800]{2,1,0:T(8,128)(2,1)} %get-tuple-element.29), calls=%async_computation.1 | async-start | bytes 917504 | tf_op jit(solution)/shard_map/all_to_all | solution.py:155
  250.3 27.9 %scatter_fusion.2 = f32[2,128,1200]{2,1,0:T(8,128)S(1)} fusion(f32[2,128,1200]{2,1,0:T(8,128)S(1)} %broadcast_in_dim.29, s32[256]{0:T(256)S(1)} %reshape.613, f32[256,1200]{1,0:T(8,128)} %bitcast.75), kind=kCustom, calls=%fused_computation.5 | custom fusion | flops 307200 | bytes 3688448 | tf_op jit(solution)/shard_map/scatter-add | solution.py:162
  279.2 2.4 gather_fusion.1
  290.6 12.4 %reduce-scatter.2.cloned.1.call-done = bf16[2,32,1200]{2,1,0:T(8,128)(2,1)} async-done(((bf16[2,128,1200]{2,1,0:T(8,128)(2,1)}), bf16[2,32,1200]{2,1,0:T(8,128)(2,1)}) %reduce-scatter.2.cloned.1.call-update) | async-done | bytes 153616 | tf_op jit(solution)/shard_map/reduce_scatter | solution.py:165
  (123 shorter events, 41.2 us)
Async XLA Ops:
  7.2 14.8 %copy-start = (bf16[1,400,400]{2,1,0:T(8,128)(2,1)S(1)}, bf16[1,400,400]{2,1,0:T(8,128)(2,1)}, u32[]{:S(2)}) copy-start(bf16[1,400,400]{2,1,0:T(8,128)(2,1)} %param.8) | copy-start | bytes 960004
  7.2 187.6 %all-gather.2.cloned.1.call-start = ((), (), s32[]{:S(2)}) async-start(), calls=%async_computation.5 | async-start | bytes 27033600 | tf_op jit(solution)/shard_map/all_gather | solution.py:97
  10.7 13.2 %copy-start.10 = (bf16[1,400,400]{2,1,0:T(8,128)(2,1)}, bf16[1,400,400]{2,1,0:T(8,128)(2,1)S(1)}, u32[]{:S(2)}) copy-start(bf16[1,400,400]{2,1,0:T(8,128)(2,1)S(1)} %get-tuple-element.31) | copy-start | bytes 960004
  13.9 10.0 %copy-start.12 = (bf16[1,400,400]{2,1,0:T(8,128)(2,1)}, bf16[1,400,400]{2,1,0:T(8,128)(2,1)S(1)}, u32[]{:S(2)}) copy-start(bf16[1,400,400]{2,1,0:T(8,128)(2,1)S(1)} %fusion.42) | copy-start | bytes 960004
  18.0 3.2 %copy-start.16 = (bf16[400,400]{1,0:T(8,128)(2,1)}, bf16[400,400]{1,0:T(8,128)(2,1)S(1)}, u32[]{:S(2)}) copy-start(bf16[400,400]{1,0:T(8,128)(2,1)S(1)} %get-tuple-element.33) | copy-start | bytes 960004
  26.2 2.1 copy-start.22
  26.2 2.1 copy-start.23
  26.2 2.1 copy-start.24
  26.3 2.2 copy-start.21
  26.3 10.9 %copy-start.25 = (f32[64]{0:T(128)S(1)}, f32[64]{0:T(128)}, u32[]{:S(2)}) copy-start(f32[64]{0:T(128)} %param.10) | copy-start | bytes 772
  27.5 17.7 %copy-start.20 = (bf16[2,128,800]{1,2,0:T(8,128)(2,1)S(1)}, bf16[2,128,800]{1,2,0:T(8,128)(2,1)}, u32[]{:S(2)}) copy-start(bf16[2,128,800]{1,2,0:T(8,128)(2,1)} %param.15) | copy-start | bytes 1228804
  29.9 18.4 %all-to-all-start = ((s32[8,2,6]{2,1,0:T(2,128)}), s32[8,2,6]{2,1,0:T(2,128)S(1)}, u32[]{:S(2)}, u32[]{:S(2)}) async-start(s32[8,2,6]{2,1,0:T(2,128)} %bitcast.22), calls=%async_computation | async-start | bytes 16384 | tf_op jit(solution)/shard_map/all_to_all | solution.py:144
  48.3 166.0 %all-to-all-start.3 = ((bf16[16,16,400]{2,1,0:T(8,128)(2,1)}), bf16[16,16,400]{2,1,0:T(8,128)(2,1)}, u32[]{:S(2)}, u32[]{:S(2)}) async-start(bf16[16,16,400]{2,1,0:T(8,128)(2,1)} %scatter_fusion.1), calls=%async_computation.3 | async-start | bytes 524288 | tf_op jit(solution)/shard_map/all_to_all | solution.py:143
  60.5 3.2 %copy-start.1 = (f32[16,16,2,400]{3,2,1,0:T(2,128)}, f32[16,16,2,400]{3,2,1,0:T(2,128)S(1)}, u32[]{:S(2)}) copy-start(f32[16,16,2,400]{3,2,1,0:T(2,128)S(1)} %reshape.574) | copy-start | bytes 2457604
  60.5 2.1 copy-start.3
  208.5 10.2 %slice-start = ((f32[16,16,2,400]{3,2,1,0:T(2,128)}), f32[16,16,2,1]{3,2,1,0:T(2,128)S(1)}, s32[]{:S(2)}) async-start(f32[16,16,2,400]{3,2,1,0:T(2,128)} %copy-done.1), calls=%async_computation.7 | async-start | bytes 524288 | tf_op jit(solution)/shard_map/jit(_roll_static)/slice | solution.py:81
  208.5 10.2 %copy-start.2 = (f32[16,16,2,399]{3,2,1,0:T(2,128)S(1)}, f32[16,16,2,399]{3,2,1,0:T(2,128)}, u32[]{:S(2)}) copy-start(f32[16,16,2,399]{3,2,1,0:T(2,128)} %slice.97) | copy-start | bytes 2451460
  214.3 17.9 %all-to-all-start.2 = ((bf16[16,16,800]{2,1,0:T(8,128)(2,1)}), bf16[16,16,800]{2,1,0:T(8,128)(2,1)}, u32[]{:S(2)}, u32[]{:S(2)}) async-start(bf16[16,16,800]{2,1,0:T(8,128)(2,1)} %scatter_fusion), calls=%async_computation.2 | async-start | bytes 917504 | tf_op jit(solution)/shard_map/all_to_all | solution.py:142
  237.0 3.2 %copy-start.4 = (f32[256,800]{1,0:T(8,128)S(1)}, f32[256,800]{1,0:T(8,128)}, u32[]{:S(2)}) copy-start(f32[256,800]{1,0:T(8,128)} %convert_element_type.272) | copy-start | bytes 2457604
  243.2 5.7 %copy-start.5 = (f32[16,16,800]{2,1,0:T(8,128)S(1)}, f32[16,16,800]{2,1,0:T(8,128)}, u32[]{:S(2)}) copy-start(f32[16,16,800]{2,1,0:T(8,128)} %get-tuple-element.28) | copy-start | bytes 2457604
  243.2 36.0 %all-to-all-start.1 = ((bf16[16,16,800]{2,1,0:T(8,128)(2,1)}), bf16[16,16,800]{2,1,0:T(8,128)(2,1)}, u32[]{:S(2)}, u32[]{:S(2)}) async-start(bf16[16,16,800]{2,1,0:T(8,128)(2,1)} %get-tuple-element.29), calls=%async_computation.1 | async-start | bytes 917504 | tf_op jit(solution)/shard_map/all_to_all | solution.py:155
  247.4 55.5 %reduce-scatter.2.cloned.1.call-start = ((), (), s32[]{:S(2)}) async-start(), calls=%async_computation.6 | async-start | bytes 819200 | tf_op jit(solution)/shard_map/reduce_scatter | solution.py:165
  279.1 6.6 %copy-start.6 = (f32[400,400]{0,1:T(8,128)S(1)}, f32[400,400]{0,1:T(8,128)}, u32[]{:S(2)}) copy-start(f32[400,400]{0,1:T(8,128)} %get-tuple-element.17) | copy-start | bytes 1920004
  279.1 6.6 %copy-start.8 = (bf16[400,400]{0,1:T(8,128)(2,1)S(1)}, bf16[400,400]{0,1:T(8,128)(2,1)}, u32[]{:S(2)}) copy-start(bf16[400,400]{0,1:T(8,128)(2,1)} %get-tuple-element.25) | copy-start | bytes 960004
  (9 other events, 12.3 us)
Sparse Core Ops, SparseCore 0:
  27.7 167.0 all-gather.1
  279.3 23.6 reduce-scatter.1
